TPU v7x, 32 devices: a whole 2x2x4 slice. The times are simulated.
32 devices in a mesh: cuts: 2 (over x), mode: 16 (over z, y, core).
Axes of the slice: x: 2, y: 2, z: 4, core: 2. Of those that a mesh axis runs over, the one named last changes fastest.
Arguments:
- stem_blocks: bfloat16 [2, 4096, 2, 256], P('cuts', 'mode'), may hold values from -6 to 6
- w1_table: bfloat16 [8, 2, 256, 256], replicated, may hold values from -0.25 to 0.25
- w2_table: bfloat16 [8, 2, 256, 256], replicated, may hold values from -0.125 to 0.125
- slice_ids: int32 [2, 2, 2], P('cuts'), may hold values from 0 to 7, as said below
- mode_perm: int32 [256], replicated, may hold values from 0 to 255, each once
Outputs:
- amplitudes: float32 [256, 16, 2, 256], P('mode', 'cuts')
Inputs may be any that keep to these rules, and one draw needn't show every extreme that they name: For each stem block b, the 2 values slice_ids[:,b,0] are distinct, and so are the 2 values slice_ids[:,b,1]. `mode_perm`: each column appears once.
All inputs are finite; a program needn't handle non-finite values.
Results may differ from a plain program's by a relative error of at most 0.0029.
Values may be sent and summed in bfloat16 or wider, within the bound.
No kernel may reach another device: no remote copies, remote signals or barrier semaphores. Data moves between devices by JAX's collectives and lax.ppermute only.
A program may use at most 64 MiB of HBM per device.

v0:
```python
import jax
import jax.numpy as jnp
from jax import lax
from jax.sharding import PartitionSpec as P


def broadcast(block, axis, source):
    block = jnp.where(lax.axis_index(axis) == source, block, jnp.zeros_like(block))
    return lax.psum(block, axis)


def widen_first(entry):
    real_part, imag_part = (entry[0], entry[1])
    upper = jnp.concatenate([real_part, imag_part], axis=1)
    lower = jnp.concatenate([-imag_part, real_part], axis=1)
    return jnp.concatenate([upper, lower], axis=0)


def widen_second(entry):
    real_part, imag_part = (entry[0], entry[1])
    first_row = jnp.concatenate([real_part, imag_part], axis=1)
    second_row = jnp.concatenate([-imag_part, real_part], axis=1)
    return jnp.stack([first_row, second_row], axis=0)


def second_step(exchanged, weight_two, contract_cols, free_cols):
    block_count, mode_count, piece_rows, _ = exchanged.shape
    pieces = exchanged.reshape(block_count, mode_count, piece_rows, 2, contract_cols, free_cols)
    wide_out = weight_two.shape[3]
    shaped = weight_two.reshape(block_count, 2, mode_count, contract_cols, wide_out)
    return jnp.einsum("nhqpcs,nphco->qso", pieces, shaped, preferred_element_type=jnp.float32)


def on_device(stem_blocks, w1_table, w2_table, slice_ids, mode_perm):
    mode_count = lax.axis_size("mode")
    row_count = stem_blocks.shape[1]
    stem_width = stem_blocks.shape[3]
    mid_width = w1_table.shape[3]
    inner_width = w2_table.shape[2]
    out_width = w2_table.shape[3]
    piece_rows = row_count // mode_count
    contract_cols = inner_width // mode_count
    free_cols = mid_width // contract_cols
    block_count = slice_ids.shape[1]
    first_all = jax.vmap(widen_first)(jnp.take(w1_table, mode_perm, axis=3))
    second_all = jax.vmap(widen_second)(w2_table)
    own_slices = slice_ids[0]
    begin = jnp.zeros((piece_rows, free_cols, 2 * out_width), jnp.float32)

    def one_block(block_index, running):
        stem_part = broadcast(stem_blocks[0], "cuts", block_index)
        slice_pair = own_slices[block_index]
        weight_one = lax.dynamic_index_in_dim(first_all, slice_pair[0], 0, keepdims=False)
        product = jnp.dot(
            stem_part.reshape(row_count, 2 * stem_width),
            weight_one,
            preferred_element_type=jnp.float32,
        ).astype(jnp.bfloat16)
        exchanged = lax.all_to_all(
            product[None, None], "mode", split_axis=2, concat_axis=1, tiled=True
        )
        weight_two = lax.dynamic_index_in_dim(second_all, slice_pair[1], 0, keepdims=True)
        return running + second_step(exchanged, weight_two, contract_cols, free_cols)

    amplitude = lax.fori_loop(0, block_count, one_block, begin)
    summed = lax.psum_scatter(amplitude, "cuts", scatter_dimension=1, tiled=True)
    return summed.reshape(piece_rows, summed.shape[1], 2, out_width)


def solution(mesh):
    placed = (P("cuts", "mode", None, None), P(), P(), P("cuts", None, None), P())
    return jax.shard_map(
        on_device,
        mesh=mesh,
        in_specs=placed,
        out_specs=P("mode", "cuts", None, None),
        check_vma=False,
    )
```

profile of v0, /device:TPU:0, one launch (start us, length us, event | category | flops | bytes accessed | tf_op | source)
XLA Modules:
  0.0 173.1 jit_solution(13787529332660151836)
XLA Ops:
  7.4 3.2 %slice_bitcast_fusion.2 = (bf16[8,256,256]{2,1,0:T(8,128)(2,1)}, bf16[8,256,256]{2,1,0:T(8,128)(2,1)}) fusion(bf16[8,2,256,256]{3,2,1,0:T(8,128)(2,1)} %param.9), kind=kLoop, calls=%fused_computation.19 | loop fusion | bytes 4194304 | tf_op jit(solution)/shard_map/vmap()/squeeze | solution.py:20
  10.6 1.1 fusion.6
  11.7 0.9 copy-done.6
  12.6 3.1 %copy.29 = bf16[8,2,256,256]{2,0,3,1:T(8,128)(2,1)} copy(bf16[8,2,256,256]{3,2,1,0:T(8,128)(2,1)S(1)} %copy-done.6) | data formatting | bytes 4194304 | tf_op args[1]
  15.7 2.4 %gather_fusion = bf16[256,8,2,256]{3,1,2,0:T(8,128)(2,1)S(1)} fusion(bf16[8,2,256,256]{2,0,3,1:T(8,128)(2,1)} %copy.29, s32[1024]{0:T(1024)S(1)} %pad_clamp_fusion), kind=kCustom, calls=%fused_computation | custom fusion | bytes 4195328 | tf_op jit(solution)/shard_map/jit(_take)/gather | solution.py:45
  18.1 0.9 select_bitcast_fusion
  19.0 1.1 slice_bitcast_fusion
  20.2 13.0 %maximum_maximum_fusion = bf16[8,512,512]{1,0,2:T(8,128)(2,1)} fusion(bf16[8,256,256]{1,0,2:T(8,128)(2,1)} %get-tuple-element.171, bf16[8,256,256]{1,0,2:T(8,128)(2,1)S(1)} %fusion.7, bf16[8,256,256]{1,0,2:T(8,128)(2,1)S(1)} %get-tuple-element.170), kind=kLoop, calls=%fused_computation.12 | loop fusion | flops 16777216 | bytes 7340032 | tf_op jit(solution)/shard_map/vmap()/concatenate | solution.py:16
  33.3 7.7 %copy.34 = bf16[8,512,512]{2,1,0:T(8,128)(2,1)} copy(bf16[8,512,512]{1,0,2:T(8,128)(2,1)} %maximum_maximum_fusion) | data formatting | bytes 8388608
  41.0 1.9 %maximum_bitcast_fusion.1 = (bf16[1,8,256,512]{3,2,0,1:T(8,128)(2,1)S(1)}, bf16[1,8,256,512]{3,2,0,1:T(8,128)(2,1)S(1)}) fusion(bf16[8,256,256]{2,1,0:T(8,128)(2,1)S(1)} %copy-done.5, bf16[8,256,256]{2,1,0:T(8,128)(2,1)} %get-tuple-element.169, bf16[8,256,256]{2,1,0:T(8,128)(2,1)S(1)} %copy-done.4), kind=kLoop, calls=%fused_computation.14 | loop fusion | flops 8388608 | bytes 7340032 | tf_op jit(solution)/shard_map/vmap()/stack | solution.py:23
  42.9 2.3 %maximum_bitcast_fusion = bf16[8,2,256,512]{3,2,1,0:T(8,128)(2,1)} fusion(bf16[1,8,256,512]{3,2,0,1:T(8,128)(2,1)S(1)} %get-tuple-element.173, bf16[1,8,256,512]{3,2,0,1:T(8,128)(2,1)S(1)} %get-tuple-element.172), kind=kLoop, calls=%fused_computation.13 | loop fusion | flops 2097152 | bytes 8388608 | tf_op jit(solution)/shard_map/vmap()/transpose | solution.py:46
  45.3 104.0 %while.14 = (s32[]{:T(128)}, f32[16,16,512]{2,1,0:T(8,128)S(1)}, bf16[1,256,2,256]{3,2,1,0:T(2,128)(2,1)S(1)}, s32[2,2]{1,0:T(2,128)S(1)}, bf16[8,512,512]{2,1,0...) while((s32[]{:T(128)}, f32[16,16,512]{2,1,0:T(8,128)S(1)}, ...), condition=%wide.region_2.3_spmd.clone, body=%wide.region_0.0_spmd.clone.sunk | while | flops 269090816 | bytes 11534731 | solution.py:65
  45.3 0.2 broadcast_select_fusion.2
  45.5 0.7 copy.52
  46.3 0.7 fusion.22
  48.9 25.5 %all-reduce.2.cloned.1.call-done = bf16[256,512]{1,0:T(8,128)(2,1)} async-done(((bf16[256,512]{1,0:T(8,128)(2,1)}), bf16[256,512]{1,0:T(8,128)(2,1)}) %all-reduce.2.cloned.1.call-update) | async-done | bytes 262160 | tf_op jit(solution)/shard_map/while/body/eval_jaxpr/psum | solution.py:9
  74.4 1.4 fusion.23
  75.8 0.4 copy.53
  76.2 0.5 broadcast.40
  76.7 2.2 %reduce.6 = bf16[256,512]{1,0:T(8,128)(2,1)S(1)} reduce(bf16[256,1,1,512]{3,2,1,0:T(2,128)(2,1)S(1)} %bitcast.79, bf16[]{:T(256)} %broadcast.40), dimensions={1,2}, to_apply=%bitcast.54.reduce_sub_computation | reduce | bytes 524290 | tf_op jit(solution)/shard_map/while
  79.0 0.9 reshape.66
  79.8 5.6 %all-to-all-start = ((bf16[16,2,4096]{2,1,0:T(2,128)(2,1)}), bf16[16,2,4096]{2,1,0:T(2,128)(2,1)S(1)}, u32[]{:S(2)}, u32[]{:S(2)}) async-start(bf16[16,2,4096]{2,1,0:T(2,128)(2,1)} %reshape.66), calls=%async_computation | async-start | bytes 524288 | tf_op jit(solution)/shard_map/while/body/eval_jaxpr/all_to_all | solution.py:59
  87.5 1.1 constant_dynamic-slice_fusion.5
  88.6 6.9 %all-to-all-done = bf16[16,2,4096]{2,1,0:T(2,128)(2,1)S(1)} async-done(((bf16[16,2,4096]{2,1,0:T(2,128)(2,1)}), bf16[16,2,4096]{2,1,0:T(2,128)(2,1)S(1)}, u32[]{:S(2)}, u32[]{:S(2)}) %all-to-all-start) | async-done | bytes 262176 | tf_op jit(solution)/shard_map/while/body/eval_jaxpr/all_to_all | solution.py:59
  95.5 0.3 reshape.67
  95.8 1.5 bitcast_reduce_fusion.2
  97.3 1.7 reshape.68
  99.0 0.7 fusion.24
  99.7 0.2 copy-done.2
  100.2 0.7 copy.52
  100.9 0.7 fusion.22
  103.5 20.2 %all-reduce.2.cloned.1.call-done = bf16[256,512]{1,0:T(8,128)(2,1)} async-done(((bf16[256,512]{1,0:T(8,128)(2,1)}), bf16[256,512]{1,0:T(8,128)(2,1)}) %all-reduce.2.cloned.1.call-update) | async-done | bytes 262160 | tf_op jit(solution)/shard_map/while/body/eval_jaxpr/psum | solution.py:9
  123.7 1.4 fusion.23
  125.2 0.4 copy.53
  125.6 0.5 broadcast.40
  126.1 2.2 %reduce.6 = bf16[256,512]{1,0:T(8,128)(2,1)S(1)} reduce(bf16[256,1,1,512]{3,2,1,0:T(2,128)(2,1)S(1)} %bitcast.79, bf16[]{:T(256)} %broadcast.40), dimensions={1,2}, to_apply=%bitcast.54.reduce_sub_computation | reduce | bytes 524290 | tf_op jit(solution)/shard_map/while
  128.3 0.9 reshape.66
  129.2 5.6 %all-to-all-start = ((bf16[16,2,4096]{2,1,0:T(2,128)(2,1)}), bf16[16,2,4096]{2,1,0:T(2,128)(2,1)S(1)}, u32[]{:S(2)}, u32[]{:S(2)}) async-start(bf16[16,2,4096]{2,1,0:T(2,128)(2,1)} %reshape.66), calls=%async_computation | async-start | bytes 524288 | tf_op jit(solution)/shard_map/while/body/eval_jaxpr/all_to_all | solution.py:59
  136.9 1.1 constant_dynamic-slice_fusion.5
  138.0 6.9 %all-to-all-done = bf16[16,2,4096]{2,1,0:T(2,128)(2,1)S(1)} async-done(((bf16[16,2,4096]{2,1,0:T(2,128)(2,1)}), bf16[16,2,4096]{2,1,0:T(2,128)(2,1)S(1)}, u32[]{:S(2)}, u32[]{:S(2)}) %all-to-all-start) | async-done | bytes 262176 | tf_op jit(solution)/shard_map/while/body/eval_jaxpr/all_to_all | solution.py:59
  144.9 0.3 reshape.67
  145.1 1.5 bitcast_reduce_fusion.2
  146.6 1.7 reshape.68
  148.3 0.7 fusion.24
  149.1 0.2 copy-done.2
  149.3 0.8 copy-done
  150.1 13.7 %reduce-scatter.2.cloned.1.call-done = f32[16,8,512]{2,1,0:T(8,128)} async-done(((f32[16,16,512]{2,1,0:T(8,128)}), f32[16,8,512]{2,1,0:T(8,128)}) %reduce-scatter.2.cloned.1.call-update) | async-done | bytes 262160 | tf_op jit(solution)/shard_map/reduce_scatter | solution.py:66
  163.8 1.8 %reshape.44 = f32[16,8,2,256]{3,2,1,0:T(2,128)} reshape(f32[16,8,512]{2,1,0:T(8,128)} %reduce-scatter.2.cloned.1.call-done) | data formatting | bytes 524288 | tf_op jit(solution)/shard_map/reshape | solution.py:67
  (30 shorter events, 0.4 us)
Async XLA Ops:
  7.4 3.2 %copy-start.3 = (bf16[8,2,256,256]{3,2,1,0:T(8,128)(2,1)S(1)}, bf16[8,2,256,256]{3,2,1,0:T(8,128)(2,1)}, u32[]{:S(2)}) copy-start(bf16[8,2,256,256]{3,2,1,0:T(8,128)(2,1)} %param.9) | copy-start | bytes 6291460
  7.4 4.3 %copy-start.7 = (s32[256]{0:T(256)S(1)}, s32[256]{0:T(256)}, u32[]{:S(2)}) copy-start(s32[256]{0:T(256)} %param.11) | copy-start | bytes 3076
  10.6 2.0 %copy-start.6 = (bf16[8,2,256,256]{3,2,1,0:T(8,128)(2,1)S(1)}, bf16[8,2,256,256]{3,2,1,0:T(8,128)(2,1)}, u32[]{:S(2)}) copy-start(bf16[8,2,256,256]{3,2,1,0:T(8,128)(2,1)} %param.8) | copy-start | bytes 6291460
  33.3 7.7 %copy-start.4 = (bf16[8,256,256]{2,1,0:T(8,128)(2,1)S(1)}, bf16[8,256,256]{2,1,0:T(8,128)(2,1)}, u32[]{:S(2)}) copy-start(bf16[8,256,256]{2,1,0:T(8,128)(2,1)} %fusion.6) | copy-start | bytes 3145732
  33.3 7.7 %copy-start.5 = (bf16[8,256,256]{2,1,0:T(8,128)(2,1)S(1)}, bf16[8,256,256]{2,1,0:T(8,128)(2,1)}, u32[]{:S(2)}) copy-start(bf16[8,256,256]{2,1,0:T(8,128)(2,1)} %get-tuple-element.168) | copy-start | bytes 3145732
  42.9 2.4 %copy-start.1 = (bf16[1,256,2,256]{3,2,1,0:T(2,128)(2,1)S(1)}, bf16[1,256,2,256]{3,2,1,0:T(2,128)(2,1)}, u32[]{:S(2)}) copy-start(bf16[1,256,2,256]{3,2,1,0:T(2,128)(2,1)} %param.7) | copy-start | bytes 786436
  42.9 2.4 %copy-start.8 = (s32[1,2,2]{2,1,0:T(2,128)S(1)}, s32[1,2,2]{2,1,0:T(2,128)}, u32[]{:S(2)}) copy-start(s32[1,2,2]{2,1,0:T(2,128)} %param.10) | copy-start | bytes 52
  45.3 29.1 %all-reduce.2.cloned.1.call-start = ((), (), s32[]{:S(2)}) async-start(), calls=%async_computation.3 | async-start | bytes 524288 | tf_op jit(solution)/shard_map/while/body/eval_jaxpr/psum | solution.py:9
  79.8 15.7 %all-to-all-start = ((bf16[16,2,4096]{2,1,0:T(2,128)(2,1)}), bf16[16,2,4096]{2,1,0:T(2,128)(2,1)S(1)}, u32[]{:S(2)}, u32[]{:S(2)}) async-start(bf16[16,2,4096]{2,1,0:T(2,128)(2,1)} %reshape.66), calls=%async_computation | async-start | bytes 524288 | tf_op jit(solution)/shard_map/while/body/eval_jaxpr/all_to_all | solution.py:59
  99.0 1.0 copy-start.2
  99.9 23.8 %all-reduce.2.cloned.1.call-start = ((), (), s32[]{:S(2)}) async-start(), calls=%async_computation.3 | async-start | bytes 524288 | tf_op jit(solution)/shard_map/while/body/eval_jaxpr/psum | solution.py:9
  129.2 15.7 %all-to-all-start = ((bf16[16,2,4096]{2,1,0:T(2,128)(2,1)}), bf16[16,2,4096]{2,1,0:T(2,128)(2,1)S(1)}, u32[]{:S(2)}, u32[]{:S(2)}) async-start(bf16[16,2,4096]{2,1,0:T(2,128)(2,1)} %reshape.66), calls=%async_computation | async-start | bytes 524288 | tf_op jit(solution)/shard_map/while/body/eval_jaxpr/all_to_all | solution.py:59
  148.3 1.0 copy-start.2
  149.3 0.8 copy-start
  149.3 14.5 %reduce-scatter.2.cloned.1.call-start = ((), (), s32[]{:S(2)}) async-start(), calls=%async_computation.2 | async-start | bytes 786432 | tf_op jit(solution)/shard_map/reduce_scatter | solution.py:66
Sparse Core Ops, SparseCore 0:
  48.5 25.8 all-reduce.1
  103.1 20.5 all-reduce.1
Sparse Core Ops, SparseCore 1:
  152.0 11.8 reduce-scatter.1
where the time goes:
time: 174 us; the launch traced here: 173 us
  waiting for transfers between devices  73.3 us (42%)
  local copies, waits for them, and re-layouts  37 us (21%)
  other arithmetic  24.2 us (14%)
  between operations  14.9 us (9%)
  starting transfers between devices  11.3 us (6%)
  loops' own time  8.19 us (5%)
  matrix products  4.28 us (2%)
    psum x2, waiting for transfers between devices, broadcast(): return lax.psum(block, axis)  45.7 us
    all_to_all x2, waiting for transfers between devices, one_block(): lax.all_to_all(product[None, None], 'mode', split_axis=2, concat_axis=1,...  13.8 us
    reduce_scatter x1, waiting for transfers between devices, on_device(): lax.psum_scatter(amplitude, 'cuts', scatter_dimension=1, tiled=True)  13.7 us
    concatenate x1, other arithmetic, widen_first(): return jnp.concatenate([upper, lower], axis=0)  13 us
    unnamed x18, local copies, waits for them, and re-layouts  12.5 us
    all_to_all x2, starting transfers between devices, one_block(): lax.all_to_all(product[None, None], 'mode', split_axis=2, concat_axis=1,...  11.2 us
    another operation x1, loops' own time, on_device(): amplitude = lax.fori_loop(0, block_count, one_block, begin)  8.19 us
    while x12, local copies, waits for them, and re-layouts  5.23 us
  transfers between devices with their start and end apart: 5, of which 5 were waited for; matrix products, arithmetic and copies ran while one was open for 2% of the time, Pallas kernels for 0%

commit v1 on v0

--- a/solution.py
+++ b/solution.py
@@ -6,7 +6,7 @@
 
 def broadcast(block, axis, source):
     block = jnp.where(lax.axis_index(axis) == source, block, jnp.zeros_like(block))
-    return lax.psum(block, axis)
+    return lax.all_gather(block, axis).sum(axis=0)
 
 
 def widen_first(entry):

time: 174 us -> 143 us (0.82)
  waiting for transfers between devices: 73.3 us -> 27.1 us
  blocking collectives: 0 us -> 18.7 us
    psum x2 -> x0, waiting for transfers between devices: 45.7 us -> none  [broadcast(): return lax.psum(block, axis)]
    all_gather x0 -> x2, blocking collectives: none -> 18.7 us  [broadcast(): return lax.all_gather(block, axis).sum(axis=0)]
    while x12 -> x14, local copies, waits for them, and re-layouts: 5.23 us -> 3.77 us
    unnamed x18 -> x17, local copies, waits for them, and re-layouts: 12.5 us -> 13.1 us
  transfers between devices with their start and end apart: 5 -> 3, of which waited for: 5 -> 3; matrix products, arithmetic and copies ran while one was open for 2% -> 2% of each run, Pallas kernels for 0% -> 0%
where the time goes in v1:
time: 143 us; the launch traced here: 142 us
  local copies, waits for them, and re-layouts  36.3 us (25%)
  waiting for transfers between devices  27.1 us (19%)
  other arithmetic  24.2 us (17%)
  blocking collectives  18.7 us (13%)
  between operations  13.5 us (9%)
  starting transfers between devices  9.74 us (7%)
  loops' own time  7.92 us (6%)
  matrix products  4.17 us (3%)
    all_gather x2, blocking collectives, broadcast(): return lax.all_gather(block, axis).sum(axis=0)  18.7 us
    all_to_all x2, waiting for transfers between devices, one_block(): lax.all_to_all(product[None, None], 'mode', split_axis=2, concat_axis=1,...  14.1 us
    unnamed x17, local copies, waits for them, and re-layouts  13.1 us
    concatenate x1, other arithmetic, widen_first(): return jnp.concatenate([upper, lower], axis=0)  13.1 us
    reduce_scatter x1, waiting for transfers between devices, on_device(): lax.psum_scatter(amplitude, 'cuts', scatter_dimension=1, tiled=True)  13 us
    all_to_all x2, starting transfers between devices, one_block(): lax.all_to_all(product[None, None], 'mode', split_axis=2, concat_axis=1,...  9.73 us
    another operation x1, loops' own time, on_device(): amplitude = lax.fori_loop(0, block_count, one_block, begin)  7.92 us
    while x2, other arithmetic  4.41 us
  transfers between devices with their start and end apart: 3, of which 3 were waited for; matrix products, arithmetic and copies ran while one was open for 2% of the time, Pallas kernels for 0%

profile of v1, /device:TPU:0, one launch (start us, length us, event | category | flops | bytes accessed | tf_op | source)
XLA Modules:
  0.0 141.5 jit_solution(9377215386235271836)
XLA Ops:
  6.5 3.2 %slice_bitcast_fusion.2 = (bf16[8,256,256]{2,1,0:T(8,128)(2,1)}, bf16[8,256,256]{2,1,0:T(8,128)(2,1)}) fusion(bf16[8,2,256,256]{3,2,1,0:T(8,128)(2,1)} %param.9), kind=kLoop, calls=%fused_computation.19 | loop fusion | bytes 4194304 | tf_op jit(solution)/shard_map/vmap()/squeeze | solution.py:20
  9.8 1.1 fusion.6
  10.8 4.5 %copy.51 = bf16[8,2,256,256]{2,0,3,1:T(8,128)(2,1)} copy(bf16[8,2,256,256]{3,2,1,0:T(8,128)(2,1)} %param.8) | data formatting | bytes 4194304 | tf_op args[1]
  15.4 2.4 %gather_fusion = bf16[256,8,2,256]{3,1,2,0:T(8,128)(2,1)S(1)} fusion(bf16[8,2,256,256]{2,0,3,1:T(8,128)(2,1)} %copy.51, s32[1024]{0:T(1024)S(1)} %pad_clamp_fusion), kind=kCustom, calls=%fused_computation | custom fusion | bytes 4195328 | tf_op jit(solution)/shard_map/jit(_take)/gather | solution.py:45
  17.8 0.9 select_bitcast_fusion
  18.7 1.1 slice_bitcast_fusion
  19.9 13.1 %maximum_maximum_fusion = bf16[8,512,512]{1,0,2:T(8,128)(2,1)} fusion(bf16[8,256,256]{1,0,2:T(8,128)(2,1)} %get-tuple-element.228, bf16[8,256,256]{1,0,2:T(8,128)(2,1)S(1)} %fusion.7, bf16[8,256,256]{1,0,2:T(8,128)(2,1)S(1)} %get-tuple-element.227), kind=kLoop, calls=%fused_computation.12 | loop fusion | flops 16777216 | bytes 7340032 | tf_op jit(solution)/shard_map/vmap()/concatenate | solution.py:16
  33.0 7.8 %copy.57 = bf16[8,512,512]{2,1,0:T(8,128)(2,1)} copy(bf16[8,512,512]{1,0,2:T(8,128)(2,1)} %maximum_maximum_fusion) | data formatting | bytes 8388608
  40.8 1.9 %maximum_bitcast_fusion.1 = (bf16[1,8,256,512]{3,2,0,1:T(8,128)(2,1)S(1)}, bf16[1,8,256,512]{3,2,0,1:T(8,128)(2,1)S(1)}) fusion(bf16[8,256,256]{2,1,0:T(8,128)(2,1)S(1)} %copy-done.5, bf16[8,256,256]{2,1,0:T(8,128)(2,1)} %get-tuple-element.226, bf16[8,256,256]{2,1,0:T(8,128)(2,1)S(1)} %copy-done.4), kind=kLoop, calls=%fused_computation.14 | loop fusion | flops 8388608 | bytes 7340032 | tf_op jit(solution)/shard_map/vmap()/stack | solution.py:23
  42.7 2.3 %maximum_bitcast_fusion = bf16[8,2,256,512]{3,2,1,0:T(8,128)(2,1)} fusion(bf16[1,8,256,512]{3,2,0,1:T(8,128)(2,1)S(1)} %get-tuple-element.230, bf16[1,8,256,512]{3,2,0,1:T(8,128)(2,1)S(1)} %get-tuple-element.229), kind=kLoop, calls=%fused_computation.13 | loop fusion | flops 2097152 | bytes 8388608 | tf_op jit(solution)/shard_map/vmap()/transpose | solution.py:46
  45.1 74.0 %while.16 = (s32[]{:T(128)}, f32[16,16,512]{2,1,0:T(8,128)S(1)}, bf16[1,256,2,256]{3,1,2,0:T(8,128)(2,1)S(1)}, s32[2,2]{1,0:T(2,128)S(1)}, bf16[8,512,512]{2,1,0...) while((s32[]{:T(128)}, f32[16,16,512]{2,1,0:T(8,128)S(1)}, ...), condition=%wide.region_2.3_spmd.clone, body=%wide.region_0.0_spmd.clone.sunk | while | flops 269090816 | bytes 12583297 | solution.py:65
  45.1 0.6 fusion.22
  47.0 9.9 %all_gather.15 = bf16[2,256,2,256]{3,1,2,0:T(8,128)(2,1)S(1)} all-gather(bf16[1,256,2,256]{3,1,2,0:T(8,128)(2,1)S(1)} %broadcast_select_fusion.2), channel_id=1, replica_groups=mesh['cuts'=2,'mode'=16] {'cuts'}, dimensions={0}, use_global_device_ids=true | all-gather | bytes 786432 | tf_op jit(solution)/shard_map/while/body/eval_jaxpr/all_gather | solution.py:9
  57.0 0.2 reduce_sum.16
  57.1 0.1 copy.74
  57.9 1.4 fusion.23
  59.3 0.4 copy.75
  59.7 0.5 broadcast.58
  60.2 2.2 %reduce.12 = bf16[256,512]{1,0:T(8,128)(2,1)S(1)} reduce(bf16[256,1,1,512]{3,2,1,0:T(2,128)(2,1)S(1)} %bitcast.75, bf16[]{:T(256)} %broadcast.58), dimensions={1,2}, to_apply=%bitcast.52.reduce_sub_computation | reduce | bytes 524290 | tf_op jit(solution)/shard_map/while
  62.4 0.9 reshape.77
  63.3 6.2 %all-to-all-start = ((bf16[16,2,4096]{2,1,0:T(2,128)(2,1)}), bf16[16,2,4096]{2,1,0:T(2,128)(2,1)S(1)}, u32[]{:S(2)}, u32[]{:S(2)}) async-start(bf16[16,2,4096]{2,1,0:T(2,128)(2,1)} %reshape.77), calls=%async_computation | async-start | bytes 524288 | tf_op jit(solution)/shard_map/while/body/eval_jaxpr/all_to_all | solution.py:59
  71.4 1.1 constant_dynamic-slice_fusion.5
  72.5 7.1 %all-to-all-done = bf16[16,2,4096]{2,1,0:T(2,128)(2,1)S(1)} async-done(((bf16[16,2,4096]{2,1,0:T(2,128)(2,1)}), bf16[16,2,4096]{2,1,0:T(2,128)(2,1)S(1)}, u32[]{:S(2)}, u32[]{:S(2)}) %all-to-all-start) | async-done | bytes 262176 | tf_op jit(solution)/shard_map/while/body/eval_jaxpr/all_to_all | solution.py:59
  79.6 0.3 reshape.78
  79.9 1.5 %bitcast_reduce_fusion.2 = bf16[256,512]{1,0:T(8,128)(2,1)S(1)} fusion(bf16[256,1,1,512]{3,2,1,0:T(2,128)(2,1)S(1)} %reshape.78), kind=kLoop, calls=%fused_computation.27.clone.1 | loop fusion | bytes 524288 | tf_op jit(solution)/shard_map/while/body/eval_jaxpr/all_to_all | solution.py:59
  81.4 1.7 %reshape.79 = bf16[16,16,2,16,16]{4,3,2,1,0:T(8,128)(2,1)S(1)} reshape(bf16[256,512]{1,0:T(8,128)(2,1)S(1)} %bitcast_reduce_fusion.2) | data formatting | bytes 524288 | tf_op jit(solution)/shard_map/reshape.42
  83.1 0.7 fusion.24
  83.8 0.2 copy-done.2
  84.0 0.6 fusion.22
  86.0 8.7 %all_gather.15 = bf16[2,256,2,256]{3,1,2,0:T(8,128)(2,1)S(1)} all-gather(bf16[1,256,2,256]{3,1,2,0:T(8,128)(2,1)S(1)} %broadcast_select_fusion.2), channel_id=1, replica_groups=mesh['cuts'=2,'mode'=16] {'cuts'}, dimensions={0}, use_global_device_ids=true | all-gather | bytes 786432 | tf_op jit(solution)/shard_map/while/body/eval_jaxpr/all_gather | solution.py:9
  94.7 0.2 reduce_sum.16
  94.9 0.1 copy.74
  95.7 1.4 fusion.23
  97.1 0.4 copy.75
  97.5 0.5 broadcast.58
  98.0 2.2 %reduce.12 = bf16[256,512]{1,0:T(8,128)(2,1)S(1)} reduce(bf16[256,1,1,512]{3,2,1,0:T(2,128)(2,1)S(1)} %bitcast.75, bf16[]{:T(256)} %broadcast.58), dimensions={1,2}, to_apply=%bitcast.52.reduce_sub_computation | reduce | bytes 524290 | tf_op jit(solution)/shard_map/while
  100.2 0.9 reshape.77
  101.1 3.5 %all-to-all-start = ((bf16[16,2,4096]{2,1,0:T(2,128)(2,1)}), bf16[16,2,4096]{2,1,0:T(2,128)(2,1)S(1)}, u32[]{:S(2)}, u32[]{:S(2)}) async-start(bf16[16,2,4096]{2,1,0:T(2,128)(2,1)} %reshape.77), calls=%async_computation | async-start | bytes 524288 | tf_op jit(solution)/shard_map/while/body/eval_jaxpr/all_to_all | solution.py:59
  106.5 1.1 constant_dynamic-slice_fusion.5
  107.6 7.0 %all-to-all-done = bf16[16,2,4096]{2,1,0:T(2,128)(2,1)S(1)} async-done(((bf16[16,2,4096]{2,1,0:T(2,128)(2,1)}), bf16[16,2,4096]{2,1,0:T(2,128)(2,1)S(1)}, u32[]{:S(2)}, u32[]{:S(2)}) %all-to-all-start) | async-done | bytes 262176 | tf_op jit(solution)/shard_map/while/body/eval_jaxpr/all_to_all | solution.py:59
  114.6 0.3 reshape.78
  114.9 1.5 %bitcast_reduce_fusion.2 = bf16[256,512]{1,0:T(8,128)(2,1)S(1)} fusion(bf16[256,1,1,512]{3,2,1,0:T(2,128)(2,1)S(1)} %reshape.78), kind=kLoop, calls=%fused_computation.27.clone.1 | loop fusion | bytes 524288 | tf_op jit(solution)/shard_map/while/body/eval_jaxpr/all_to_all | solution.py:59
  116.4 1.7 %reshape.79 = bf16[16,16,2,16,16]{4,3,2,1,0:T(8,128)(2,1)S(1)} reshape(bf16[256,512]{1,0:T(8,128)(2,1)S(1)} %bitcast_reduce_fusion.2) | data formatting | bytes 524288 | tf_op jit(solution)/shard_map/reshape.42
  118.1 0.7 fusion.24
  118.8 0.2 copy-done.2
  119.1 0.8 copy-done
  119.9 13.0 %reduce-scatter.2.cloned.1.call-done = f32[16,8,512]{2,1,0:T(8,128)} async-done(((f32[16,16,512]{2,1,0:T(8,128)}), f32[16,8,512]{2,1,0:T(8,128)}) %reduce-scatter.2.cloned.1.call-update) | async-done | bytes 262160 | tf_op jit(solution)/shard_map/reduce_scatter | solution.py:66
  132.9 1.8 %reshape.56 = f32[16,8,2,256]{3,2,1,0:T(2,128)} reshape(f32[16,8,512]{2,1,0:T(8,128)} %reduce-scatter.2.cloned.1.call-done) | data formatting | bytes 524288 | tf_op jit(solution)/shard_map/reshape | solution.py:67
  (31 shorter events, 0.2 us)
Async XLA Ops:
  6.5 3.2 %copy-start.3 = (bf16[8,2,256,256]{3,2,1,0:T(8,128)(2,1)S(1)}, bf16[8,2,256,256]{3,2,1,0:T(8,128)(2,1)}, u32[]{:S(2)}) copy-start(bf16[8,2,256,256]{3,2,1,0:T(8,128)(2,1)} %param.9) | copy-start | bytes 6291460
  6.5 4.3 %copy-start.7 = (s32[256]{0:T(256)S(1)}, s32[256]{0:T(256)}, u32[]{:S(2)}) copy-start(s32[256]{0:T(256)} %param.11) | copy-start | bytes 3076
  6.5 126.3 %reduce-scatter.2.cloned.1.call-start = ((), (), s32[]{:S(2)}) async-start(), calls=%async_computation.2 | async-start | bytes 786432 | tf_op jit(solution)/shard_map/reduce_scatter | solution.py:66
  33.0 7.8 %copy-start.6 = (bf16[1,256,2,256]{3,2,1,0:T(2,128)(2,1)S(1)}, bf16[1,256,2,256]{3,2,1,0:T(2,128)(2,1)}, u32[]{:S(2)}) copy-start(bf16[1,256,2,256]{3,2,1,0:T(2,128)(2,1)} %param.7) | copy-start | bytes 786436
  33.0 7.8 %copy-start.4 = (bf16[8,256,256]{2,1,0:T(8,128)(2,1)S(1)}, bf16[8,256,256]{2,1,0:T(8,128)(2,1)}, u32[]{:S(2)}) copy-start(bf16[8,256,256]{2,1,0:T(8,128)(2,1)} %fusion.6) | copy-start | bytes 3145732
  33.0 7.8 %copy-start.5 = (bf16[8,256,256]{2,1,0:T(8,128)(2,1)S(1)}, bf16[8,256,256]{2,1,0:T(8,128)(2,1)}, u32[]{:S(2)}) copy-start(bf16[8,256,256]{2,1,0:T(8,128)(2,1)} %get-tuple-element.225) | copy-start | bytes 3145732
  42.7 2.4 %copy-start.8 = (s32[1,2,2]{2,1,0:T(2,128)S(1)}, s32[1,2,2]{2,1,0:T(2,128)}, u32[]{:S(2)}) copy-start(s32[1,2,2]{2,1,0:T(2,128)} %param.10) | copy-start | bytes 52
  45.1 1.9 %copy-start.1 = (bf16[1,256,2,256]{3,1,2,0:T(8,128)(2,1)}, bf16[1,256,2,256]{3,1,2,0:T(8,128)(2,1)S(1)}, u32[]{:S(2)}) copy-start(bf16[1,256,2,256]{3,1,2,0:T(8,128)(2,1)S(1)} %get-tuple-element.300) | copy-start | bytes 786436 | tf_op jit(solution)/shard_map/while
  63.3 16.3 %all-to-all-start = ((bf16[16,2,4096]{2,1,0:T(2,128)(2,1)}), bf16[16,2,4096]{2,1,0:T(2,128)(2,1)S(1)}, u32[]{:S(2)}, u32[]{:S(2)}) async-start(bf16[16,2,4096]{2,1,0:T(2,128)(2,1)} %reshape.77), calls=%async_computation | async-start | bytes 524288 | tf_op jit(solution)/shard_map/while/body/eval_jaxpr/all_to_all | solution.py:59
  83.1 1.0 copy-start.2
  84.0 1.9 %copy-start.1 = (bf16[1,256,2,256]{3,1,2,0:T(8,128)(2,1)}, bf16[1,256,2,256]{3,1,2,0:T(8,128)(2,1)S(1)}, u32[]{:S(2)}) copy-start(bf16[1,256,2,256]{3,1,2,0:T(8,128)(2,1)S(1)} %get-tuple-element.300) | copy-start | bytes 786436 | tf_op jit(solution)/shard_map/while
  101.1 13.5 %all-to-all-start = ((bf16[16,2,4096]{2,1,0:T(2,128)(2,1)}), bf16[16,2,4096]{2,1,0:T(2,128)(2,1)S(1)}, u32[]{:S(2)}, u32[]{:S(2)}) async-start(bf16[16,2,4096]{2,1,0:T(2,128)(2,1)} %reshape.77), calls=%async_computation | async-start | bytes 524288 | tf_op jit(solution)/shard_map/while/body/eval_jaxpr/all_to_all | solution.py:59
  118.1 1.0 copy-start.2
  119.1 0.8 copy-start
Sparse Core Ops, SparseCore 0:
  120.0 12.8 reduce-scatter.1
